TPU v7x, 128 devices: a whole 4x4x4 slice. The times are simulated.
128 devices in a mesh: wide: 16 (over z, y), narrow: 8 (over x, core).
Axes of the slice: x: 4, y: 4, z: 4, core: 2. Of those that a mesh axis runs over, the one named last changes fastest.
Arguments:
- matrix_panel: float32 [8, 16777216], P(None, ('wide', 'narrow')), may hold values from -6 to 6
- sign_bits: int32 [16777216], P(('wide', 'narrow')), may hold values from 0 to 1
Outputs:
- mixed_panel: float32 [8, 16777216], P(None, ('wide', 'narrow'))
All inputs are finite; a program needn't handle non-finite values.
Results may differ from a plain program's by a relative error of at most 0.000086.
Values sent between devices are 32-bit elements; how exact they have to be, the bound alone decides.
No kernel may reach another device: no remote copies, remote signals or barrier semaphores. Data moves between devices by JAX's collectives and lax.ppermute only.
A program may use at most 64 MiB of HBM per device.

v0:
```python
import math

import jax
import jax.numpy as jnp
from jax import lax
from jax.sharding import PartitionSpec as P


def swapped(shard, axis, distance):
    return lax.ppermute(shard, axis, [(i, i ^ 1 << distance) for i in range(lax.axis_size(axis))])


def hadamard_table(order):
    index = jnp.arange(order, dtype=jnp.int32)
    common = jnp.bitwise_and(index[:, None], index[None, :])
    parity = jnp.zeros((order, order), jnp.int32)
    for level in range(max(order.bit_length() - 1, 0)):
        parity = parity + jnp.bitwise_and(jnp.right_shift(common, level), 1)
    return (1 - 2 * jnp.bitwise_and(parity, 1)).astype(jnp.float32)


def local_transform(values):
    columns, length = values.shape
    factors = []
    remain = length
    while remain > 1:
        factor = min(128, remain)
        factors.insert(0, factor)
        remain = remain // factor
    before = 1
    for factor in factors:
        after = length // (before * factor)
        table = hadamard_table(factor)
        if after > 1:
            shaped = values.reshape(columns, before, factor, after)
            shaped = jnp.einsum("cafb,gf->cagb", shaped, table, precision=lax.Precision.HIGHEST)
        else:
            shaped = values.reshape(columns, before, factor)
            shaped = jnp.einsum("caf,gf->cag", shaped, table, precision=lax.Precision.HIGHEST)
        values = shaped.reshape(columns, length)
        before = before * factor
    return values


def body(matrix_panel, sign_bits):
    signed = matrix_panel * (2 * sign_bits - 1).astype(jnp.float32)[None, :]
    current = local_transform(signed)
    columns, length = current.shape
    wide_count = lax.axis_size("wide")
    narrow_count = lax.axis_size("narrow")
    position = lax.axis_index("narrow")
    for level in range(narrow_count.bit_length() - 1):
        partner = swapped(current, "narrow", level)
        upper_half = jnp.bitwise_and(jnp.right_shift(position, level), 1) == 1
        current = jnp.where(upper_half, partner - current, current + partner)
    wide_table = hadamard_table(wide_count)
    blocks = current.reshape(columns, wide_count, length // wide_count)
    mixed = jnp.einsum(
        "cwr,vw->cvr",
        lax.all_to_all(blocks, "wide", split_axis=1, concat_axis=1, tiled=True),
        wide_table,
        precision=lax.Precision.HIGHEST,
    )
    current = lax.all_to_all(mixed, "wide", split_axis=1, concat_axis=1, tiled=True).reshape(
        columns, length
    )
    scale = jnp.float32(1.0 / math.sqrt(length * wide_count * narrow_count))
    return current * scale


def solution(mesh):
    in_specs = (P(None, ("wide", "narrow")), P(("wide", "narrow")))
    out_specs = P(None, ("wide", "narrow"))
    return jax.shard_map(body, mesh=mesh, in_specs=in_specs, out_specs=out_specs, check_vma=False)
```

profile of v0, /device:TPU:0, one launch (start us, length us, event | category | flops | bytes accessed | tf_op | source)
XLA Modules:
  0.0 355.6 jit_solution(16010209567714988708)
XLA Ops:
  0.0 1.1 add_convert_fusion
  1.1 2.7 broadcast_multiply_fusion.1
  3.8 6.3 %fusion.5 = f32[8,8,128,128]{3,1,2,0:T(8,128)S(1)} fusion(f32[8,8,16384]{2,0,1:T(8,128)S(1)} %bitcast.37), kind=kOutput, calls=%fused_computation.10 | convolution fusion | flops 100664128 | bytes 8388608 | tf_op jit(solution)/shard_map/cafb,gf->cagb/dot_general | solution.py:36
  10.1 4.1 %fusion.1 = f32[128,8,8,128]{3,0,2,1:T(8,128)S(1)} fusion(f32[8,8,128,128]{3,1,2,0:T(8,128)S(1)} %fusion.5), kind=kOutput, calls=%fused_computation.3 | convolution fusion | flops 1611022336 | bytes 8388608 | tf_op jit(solution)/shard_map/cafb,gf->cagb/dot_general | solution.py:36
  14.2 3.7 %convolution_bitcast_fusion.1 = f32[1,8,1024,128]{3,2,1,0:T(8,128)S(1)} fusion(f32[8,1024,128]{2,1,0:T(8,128)S(1)} %bitcast.38), kind=kOutput, calls=%fused_computation.11 | convolution fusion | flops 1611022336 | bytes 8388608 | tf_op jit(solution)/shard_map/caf,gf->cag/dot_general | solution.py:39
  17.9 0.0 copy-start
  17.9 4.4 %copy.22 = f32[1,8,1024,128]{3,1,2,0:T(8,128)} copy(f32[1,8,1024,128]{3,2,1,0:T(8,128)S(1)} %convolution_bitcast_fusion.1) | data formatting | bytes 8388608
  22.3 0.0 copy-done
  22.3 0.0 collective-permute-start
  22.3 7.5 %collective-permute-done = f32[8,131072]{1,0:T(8,128)} collective-permute-done((f32[8,131072]{1,0:T(8,128)}, f32[8,131072]{1,0:T(8,128)}, u32[]{:S(2)}, u32[]{:S(2)}) %collective-permute-start) | collective-permute-done | bytes 4194336 | tf_op jit(solution)/shard_map/ppermute | solution.py:10
  29.8 8.0 %add_select_fusion.2 = f32[8,131072]{1,0:T(8,128)} fusion(f32[8,131072]{1,0:T(8,128)} %collective-permute-done, pred[]{:T(512)S(6)} %eq.11, f32[1,8,1024,128]{3,2,1,0:T(8,128)} %copy-done), kind=kLoop, calls=%fused_computation.9 | loop fusion | flops 3145728 | bytes 12582913 | tf_op jit(solution)/shard_map/jit(_where)/select_n | solution.py:55
  37.8 1.6 collective-permute-start.1
  39.4 91.3 %collective-permute-done.1 = f32[8,131072]{1,0:T(8,128)} collective-permute-done((f32[8,131072]{1,0:T(8,128)}, f32[8,131072]{1,0:T(8,128)}, u32[]{:S(2)}, u32[]{:S(2)}) %collective-permute-start.1) | collective-permute-done | bytes 4194336 | tf_op jit(solution)/shard_map/ppermute | solution.py:10
  130.8 5.9 %add_select_fusion.1 = f32[8,131072]{1,0:T(8,128)} fusion(f32[8,131072]{1,0:T(8,128)} %add_select_fusion.2, f32[8,131072]{1,0:T(8,128)} %collective-permute-done.1, pred[]{:T(512)S(6)} %eq.10), kind=kLoop, calls=%fused_computation.8 | loop fusion | flops 3145728 | bytes 12582913 | tf_op jit(solution)/shard_map/jit(_where)/select_n | solution.py:55
  136.7 3.1 collective-permute-start.2
  139.8 90.4 %collective-permute-done.2 = f32[8,131072]{1,0:T(8,128)} collective-permute-done((f32[8,131072]{1,0:T(8,128)}, f32[8,131072]{1,0:T(8,128)}, u32[]{:S(2)}, u32[]{:S(2)}) %collective-permute-start.2) | collective-permute-done | bytes 4194336 | tf_op jit(solution)/shard_map/ppermute | solution.py:10
  230.3 3.9 %add_select_fusion = f32[8,131072]{1,0:T(8,128)S(1)} fusion(f32[8,131072]{1,0:T(8,128)} %add_select_fusion.1, f32[8,131072]{1,0:T(8,128)} %collective-permute-done.2, pred[]{:T(512)S(6)} %eq.9), kind=kLoop, calls=%fused_computation.7 | loop fusion | flops 3145728 | bytes 12582913 | tf_op jit(solution)/shard_map/jit(_where)/select_n | solution.py:55
  234.2 58.8 %all_to_all.10 = f32[8,16,8192]{2,0,1:T(8,128)S(1)} all-to-all(f32[8,16,8192]{2,0,1:T(8,128)S(1)} %bitcast.36), channel_id=1, replica_groups=mesh['wide'=16,'narrow'=8] {'wide'}, dimensions={1} | all-to-all | bytes 8388608 | tf_op jit(solution)/shard_map/all_to_all | solution.py:60
  292.9 5.6 %convolution_bitcast_fusion = f32[8,16,8192]{2,1,0:T(8,128)S(1)} fusion(f32[8,16,8192]{2,0,1:T(8,128)S(1)} %all_to_all.10), kind=kOutput, calls=%fused_computation | convolution fusion | flops 201330688 | bytes 8388608 | tf_op jit(solution)/shard_map/cwr,vw->cvr/dot_general | solution.py:58
  298.5 2.4 copy.8
  300.9 52.3 %all_to_all.11 = f32[8,16,8192]{2,0,1:T(8,128)S(1)} all-to-all(f32[8,16,8192]{2,0,1:T(8,128)S(1)} %copy.8), channel_id=1, replica_groups=mesh['wide'=16,'narrow'=8] {'wide'}, dimensions={1} | all-to-all | bytes 8388608 | tf_op jit(solution)/shard_map/all_to_all | solution.py:64
  353.3 2.3 broadcast_multiply_fusion
Async XLA Ops:
  17.9 4.5 %copy-start = (f32[1,8,1024,128]{3,2,1,0:T(8,128)}, f32[1,8,1024,128]{3,2,1,0:T(8,128)S(1)}, u32[]{:S(2)}) copy-start(f32[1,8,1024,128]{3,2,1,0:T(8,128)S(1)} %convolution_bitcast_fusion.1) | copy-start | bytes 12582916
  22.3 7.5 %collective-permute-start = (f32[8,131072]{1,0:T(8,128)}, f32[8,131072]{1,0:T(8,128)}, u32[]{:S(2)}, u32[]{:S(2)}) collective-permute-start(f32[8,131072]{1,0:T(8,128)} %bitcast.35), channel_id=1, source_target_pairs={{0,1},{1,0},{2,3},{3,2},{4,5},{5,4},{6,7},{7,6},{8,9},{9,8},{10,11... | collective-permute-start | bytes 12582920 | tf_op jit(solution)/shard_map/ppermute | solution.py:10
  37.8 92.9 %collective-permute-start.1 = (f32[8,131072]{1,0:T(8,128)}, f32[8,131072]{1,0:T(8,128)}, u32[]{:S(2)}, u32[]{:S(2)}) collective-permute-start(f32[8,131072]{1,0:T(8,128)} %add_select_fusion.2), channel_id=1, source_target_pairs={{0,2},{1,3},{2,0},{3,1},{4,6},{5,7},{6,4},{7,5},{8,10},{9,11},{10,... | collective-permute-start | bytes 12582920 | tf_op jit(solution)/shard_map/ppermute | solution.py:10
  136.7 93.6 %collective-permute-start.2 = (f32[8,131072]{1,0:T(8,128)}, f32[8,131072]{1,0:T(8,128)}, u32[]{:S(2)}, u32[]{:S(2)}) collective-permute-start(f32[8,131072]{1,0:T(8,128)} %add_select_fusion.1), channel_id=1, source_target_pairs={{0,4},{1,5},{2,6},{3,7},{4,0},{5,1},{6,2},{7,3},{8,12},{9,13},{10,... | collective-permute-start | bytes 12582920 | tf_op jit(solution)/shard_map/ppermute | solution.py:10
where the time goes:
time: 356 us
  waiting for transfers between devices  189 us (53%)
  blocking collectives  111 us (31%)
  other arithmetic  24 us (7%)
  matrix products  19.6 us (6%)
  local copies, waits for them, and re-layouts  6.88 us (2%)
  starting transfers between devices  4.75 us (1%)
    ppermute x3, waiting for transfers between devices, swapped(): lax.ppermute(shard, axis, [(i, i ^ 1 << distance) for i in range(lax.axis...  189 us
    all_to_all x1, blocking collectives, body(): lax.all_to_all(blocks, 'wide', split_axis=1, concat_axis=1, tiled=True)  58.8 us
    all_to_all x1, blocking collectives, body(): lax.all_to_all(mixed, 'wide', split_axis=1, concat_axis=1, tiled=True)  52.3 us
    select_n x3, other arithmetic, body(): current = jnp.where(upper_half, partner - current, current + partner)  17.8 us
    dot_general x2, matrix products, local_transform(): jnp.einsum('cafb,gf->cagb', shaped, table, precision=lax.Precision.HIGHEST)  10.4 us
  transfers between devices with their start and end apart: 3, of which 3 were waited for; matrix products, arithmetic and copies ran while one was open for 0% of the time, Pallas kernels for 0%

commit v1 on v0

v1 whole, which is shorter than its diff:
```python
import math

import jax
import jax.numpy as jnp
from jax import lax
from jax.sharding import PartitionSpec as P


def hadamard_table(order):
    index = jnp.arange(order, dtype=jnp.int32)
    common = jnp.bitwise_and(index[:, None], index[None, :])
    parity = jnp.zeros((order, order), jnp.int32)
    for level in range(max(order.bit_length() - 1, 0)):
        parity = parity + jnp.bitwise_and(jnp.right_shift(common, level), 1)
    return (1 - 2 * jnp.bitwise_and(parity, 1)).astype(jnp.float32)


def local_transform(values):
    columns, length = values.shape
    factors = []
    remain = length
    while remain > 1:
        factor = min(128, remain)
        factors.insert(0, factor)
        remain = remain // factor
    before = 1
    for factor in factors:
        after = length // (before * factor)
        table = hadamard_table(factor)
        if after > 1:
            shaped = values.reshape(columns, before, factor, after)
            shaped = jnp.einsum("cafb,gf->cagb", shaped, table, precision=lax.Precision.HIGHEST)
        else:
            shaped = values.reshape(columns, before, factor)
            shaped = jnp.einsum("caf,gf->cag", shaped, table, precision=lax.Precision.HIGHEST)
        values = shaped.reshape(columns, length)
        before = before * factor
    return values


AXES = ("wide", "narrow")


def body(matrix_panel, sign_bits):
    signed = matrix_panel * (2 * sign_bits - 1).astype(jnp.float32)[None, :]
    current = local_transform(signed)
    columns, length = current.shape
    devices = lax.axis_size("wide") * lax.axis_size("narrow")
    blocks = current.reshape(columns, devices, length // devices)
    gathered = lax.all_to_all(blocks, AXES, split_axis=1, concat_axis=1, tiled=True)
    mixed = jnp.einsum(
        "csr,vs->cvr", gathered, hadamard_table(devices), precision=lax.Precision.HIGHEST
    )
    current = lax.all_to_all(mixed, AXES, split_axis=1, concat_axis=1, tiled=True)
    scale = jnp.float32(1.0 / math.sqrt(length * devices))
    return current.reshape(columns, length) * scale


def solution(mesh):
    in_specs = (P(None, AXES), P(AXES))
    out_specs = P(None, AXES)
    return jax.shard_map(body, mesh=mesh, in_specs=in_specs, out_specs=out_specs, check_vma=False)
```

time: 356 us -> 161 us (0.45)
  waiting for transfers between devices: 189 us -> 0 us
  other arithmetic: 24 us -> 6.29 us
  blocking collectives: 111 us -> 121 us
  local copies, waits for them, and re-layouts: 6.88 us -> 11.9 us
  starting transfers between devices: 4.75 us -> 0 us
    ppermute x3 -> x0, waiting for transfers between devices: 189 us -> none  [swapped(): lax.ppermute(shard, axis, [(i, i ^ 1 << distance) for i in range(lax.axis...]
    select_n x3 -> x0, other arithmetic: 17.8 us -> none  [body(): current = jnp.where(upper_half, partner - current, current + partner)]
    all_to_all x2, blocking collectives: 111 us -> 121 us  [the longest x1 63.8 us: body(): lax.all_to_all(blocks, AXES, split_axis=1, concat_axis=1, tiled=True)]
    another operation x0 -> x2, local copies, waits for them, and re-layouts: none -> 9.49 us  [body(): blocks = current.reshape(columns, devices, length // devices)]
    ppermute x3 -> x0, starting transfers between devices: 4.75 us -> none  [swapped(): lax.ppermute(shard, axis, [(i, i ^ 1 << distance) for i in range(lax.axis...]
    unnamed x3 -> x0, local copies, waits for them, and re-layouts: 4.45 us -> none
  transfers between devices with their start and end apart: 3 -> 0, of which waited for: 3 -> 0; matrix products, arithmetic and copies ran while one was open for 0% -> 0% of each run, Pallas kernels for 0% -> 0%
where the time goes in v1:
time: 161 us
  blocking collectives  121 us (75%)
  matrix products  21.7 us (13%)
  local copies, waits for them, and re-layouts  11.9 us (7%)
  other arithmetic  6.29 us (4%)
    all_to_all x1, blocking collectives, body(): lax.all_to_all(blocks, AXES, split_axis=1, concat_axis=1, tiled=True)  63.8 us
    all_to_all x1, blocking collectives, body(): lax.all_to_all(mixed, AXES, split_axis=1, concat_axis=1, tiled=True)  56.8 us
    dot_general x2, matrix products, local_transform(): jnp.einsum('cafb,gf->cagb', shaped, table, precision=lax.Precision.HIGHEST)  10.6 us
    another operation x2, local copies, waits for them, and re-layouts, body(): blocks = current.reshape(columns, devices, length // devices)  9.49 us
    dot_general x1, matrix products, body(): jnp.einsum('csr,vs->cvr', gathered, hadamard_table(devices), precision=la...  5.9 us
    dot_general x1, matrix products, local_transform(): jnp.einsum('caf,gf->cag', shaped, table, precision=lax.Precision.HIGHEST)  5.21 us

profile of v1, /device:TPU:0, one launch (start us, length us, event | category | flops | bytes accessed | tf_op | source)
XLA Modules:
  0.0 160.6 jit_solution(17547740681972419085)
XLA Ops:
  0.0 1.1 add_convert_fusion
  1.1 2.7 %broadcast_multiply_fusion.1 = f32[8,131072]{1,0:T(8,128)S(1)} fusion(f32[8,131072]{1,0:T(8,128)} %param.2, f32[131072]{0:T(1024)S(1)} %add_convert_fusion), kind=kLoop, calls=%fused_computation.9 | loop fusion | flops 1048576 | bytes 8912896 | tf_op jit(solution)/shard_map/mul | solution.py:45
  3.8 6.3 %fusion.6 = f32[8,8,128,128]{3,1,2,0:T(8,128)S(1)} fusion(f32[8,8,16384]{2,0,1:T(8,128)S(1)} %bitcast.27), kind=kOutput, calls=%fused_computation.6 | convolution fusion | flops 100664128 | bytes 8388608 | tf_op jit(solution)/shard_map/cafb,gf->cagb/dot_general | solution.py:32
  10.1 4.3 %fusion.2 = f32[128,8,8,128]{3,0,2,1:T(8,128)S(1)} fusion(f32[8,8,128,128]{3,1,2,0:T(8,128)S(1)} %fusion.6), kind=kOutput, calls=%fused_computation.2 | convolution fusion | flops 1611022336 | bytes 8388608 | tf_op jit(solution)/shard_map/cafb,gf->cagb/dot_general | solution.py:32
  14.4 5.2 %fusion.14 = f32[8,1024,128]{2,1,0:T(8,128)} fusion(f32[8,1024,128]{2,1,0:T(8,128)S(1)} %bitcast.28), kind=kOutput, calls=%fused_computation.13 | convolution fusion | flops 1611022336 | bytes 8388608 | tf_op jit(solution)/shard_map/caf,gf->cag/dot_general | solution.py:35
  19.7 4.9 %reshape_reshape.11 = f32[8,128,1024]{2,1,0:T(8,128)} reshape(f32[8,1024,128]{2,1,0:T(8,128)} %fusion.14) | data formatting | bytes 8388608 | tf_op jit(solution)/shard_map/reshape;reshape | solution.py:49
  24.5 4.6 %copy.7 = f32[8,128,1024]{2,0,1:T(8,128)S(1)} copy(f32[8,128,1024]{2,1,0:T(8,128)} %reshape_reshape.11) | data formatting | bytes 8388608 | tf_op jit(solution)/shard_map/reshape;reshape | solution.py:49
  29.1 63.8 %all_to_all.10 = f32[8,128,1024]{2,0,1:T(8,128)S(1)} all-to-all(f32[8,128,1024]{2,0,1:T(8,128)S(1)} %copy.7), channel_id=1, replica_groups=mesh['wide'=16,'narrow'=8] {'wide','narrow'}, dimensions={1} | all-to-all | bytes 8388608 | tf_op jit(solution)/shard_map/all_to_all | solution.py:50
  93.0 5.9 %fusion.9 = f32[8,128,1024]{2,1,0:T(8,128)S(1)} fusion(f32[8,128,1024]{2,0,1:T(8,128)S(1)} %all_to_all.10), kind=kOutput, calls=%fused_computation.7 | convolution fusion | flops 1611022336 | bytes 8388608 | tf_op jit(solution)/shard_map/csr,vs->cvr/dot_general | solution.py:51
  98.9 2.4 %copy.9 = f32[8,128,1024]{2,0,1:T(8,128)S(1)} copy(f32[8,128,1024]{2,1,0:T(8,128)S(1)} %fusion.9) | data formatting | bytes 8388608 | tf_op jit(solution)/shard_map/csr,vs->cvr/transpose | solution.py:51
  101.3 56.8 %all_to_all.11 = f32[8,128,1024]{2,0,1:T(8,128)S(1)} all-to-all(f32[8,128,1024]{2,0,1:T(8,128)S(1)} %copy.9), channel_id=1, replica_groups=mesh['wide'=16,'narrow'=8] {'wide','narrow'}, dimensions={1} | all-to-all | bytes 8388608 | tf_op jit(solution)/shard_map/all_to_all | solution.py:54
  158.1 2.5 %broadcast_multiply_fusion = f32[8,128,1024]{2,0,1:T(8,128)} fusion(f32[8,128,1024]{2,0,1:T(8,128)S(1)} %all_to_all.11), kind=kLoop, calls=%fused_computation.8 | loop fusion | flops 1048576 | bytes 8388608 | tf_op jit(solution)/shard_map/mul | solution.py:56

commit v2 on v1

v2 whole, which is shorter than its diff:
```python
import math

import jax
import jax.numpy as jnp
from jax import lax
from jax.experimental import pallas as pl
from jax.experimental.pallas import tpu as pltpu
from jax.sharding import PartitionSpec as P

AXES = ("wide", "narrow")
LANES = 128


def hadamard_table(order):
    index = jnp.arange(order, dtype=jnp.int32)
    common = jnp.bitwise_and(index[:, None], index[None, :])
    parity = jnp.zeros((order, order), jnp.int32)
    for level in range(max(order.bit_length() - 1, 0)):
        parity = parity + jnp.bitwise_and(jnp.right_shift(common, level), 1)
    return (1 - 2 * jnp.bitwise_and(parity, 1)).astype(jnp.float32)


def butterfly(vals):
    n = len(vals)
    half = 1
    while half < n:
        out = list(vals)
        for i in range(n):
            if not i & half:
                a, b = vals[i], vals[i | half]
                out[i] = a + b
                out[i | half] = a - b
        vals = out
        half *= 2
    return vals


def radix_pass(src, dst, rows, low, bits, pre=None, post=None):
    span = 1 << bits
    stride = 1 << low

    def step(g, carry):
        base = (g // stride) * (stride * span) + g % stride
        vals = [src[base + j * stride] for j in range(span)]
        if pre is not None:
            vals = pre(vals, base, stride)
        vals = butterfly(vals)
        if post is not None:
            vals = [post(v) for v in vals]
        for j in range(span):
            dst[base + j * stride] = vals[j]
        return carry

    lax.fori_loop(0, rows // span, step, 0)


def pre_kernel(x_ref, s_ref, h_ref, o_ref):
    rows = x_ref.shape[0]
    table = h_ref[...]

    def signed_lanes(vals, base, stride):
        out = []
        for j, v in enumerate(vals):
            sign = s_ref[pl.ds(base + j * stride, 1), :].astype(jnp.float32) * 2.0 - 1.0
            out.append(v * sign)
        block = jnp.concatenate(out, axis=0)
        mixed = jnp.dot(block, table, precision=lax.Precision.HIGHEST,
                        preferred_element_type=jnp.float32)
        cols = vals[0].shape[0]
        return [mixed[j * cols:(j + 1) * cols] for j in range(len(vals))]

    radix_pass(x_ref, o_ref, rows, 3, 4, pre=signed_lanes)
    radix_pass(o_ref, o_ref, rows, 7, 3)


def mid_kernel(x_ref, o_ref, *, scale):
    rows = x_ref.shape[0]
    radix_pass(x_ref, o_ref, rows, 0, 4)
    radix_pass(o_ref, o_ref, rows, 4, 3)
    radix_pass(o_ref, o_ref, rows, 7, 3, post=lambda v: v * scale)


def vmem_call(kernel, out_shape, n_in):
    return pl.pallas_call(
        kernel,
        out_shape=out_shape,
        in_specs=[pl.BlockSpec(memory_space=pltpu.VMEM)] * n_in,
        out_specs=pl.BlockSpec(memory_space=pltpu.VMEM),
        compiler_params=pltpu.CompilerParams(vmem_limit_bytes=48 * 1024 * 1024),
    )


def body(matrix_panel, sign_bits):
    columns, length = matrix_panel.shape
    devices = lax.axis_size("wide") * lax.axis_size("narrow")
    rows = length // LANES
    x = matrix_panel.reshape(columns, rows, LANES).transpose(1, 0, 2)
    signs = sign_bits.reshape(rows, LANES)
    shape = jax.ShapeDtypeStruct((rows, columns, LANES), jnp.float32)
    y = vmem_call(pre_kernel, shape, 3)(x, signs, hadamard_table(LANES))
    blocks = y.reshape(devices, rows // devices, columns, LANES)
    gathered = lax.all_to_all(blocks, AXES, 0, 0, tiled=True).reshape(rows, columns, LANES)
    scale = 1.0 / math.sqrt(length * devices)
    mixed = vmem_call(lambda a, b: mid_kernel(a, b, scale=scale), shape, 1)(gathered)
    back = lax.all_to_all(mixed.reshape(blocks.shape), AXES, 0, 0, tiled=True)
    return back.reshape(rows, columns, LANES).transpose(1, 0, 2).reshape(columns, length)


def solution(mesh):
    in_specs = (P(None, AXES), P(AXES))
    out_specs = P(None, AXES)
    return jax.shard_map(body, mesh=mesh, in_specs=in_specs, out_specs=out_specs, check_vma=False)
```

time: 161 us -> 151 us (0.938)
  Pallas kernels: 0 us -> 25.9 us
  matrix products: 21.7 us -> 0 us
  local copies, waits for them, and re-layouts: 11.9 us -> 3.05 us
  other arithmetic: 6.29 us -> 0.06 us
    pallas_call x0 -> x2, Pallas kernels: none -> 25.9 us  [the longest x1 18.4 us: body(): y = vmem_call(pre_kernel, shape, 3)(x, signs, hadamard_table(LANES))]
    dot_general x4 -> x0, matrix products: 21.7 us -> none  [the longest x2 10.6 us: local_transform(): jnp.einsum('cafb,gf->cagb', shaped, table, precision=lax.Precision.HIGHEST)]
    another operation x2 -> x0, local copies, waits for them, and re-layouts: 9.49 us -> none  [body(): blocks = current.reshape(columns, devices, length // devices)]
    mul x2 -> x0, other arithmetic: 5.19 us -> none  [the longest x1 2.73 us: body(): signed = matrix_panel * (2 * sign_bits - 1).astype(jnp.float32)[None, :]]
    unnamed x0 -> x3, local copies, waits for them, and re-layouts: none -> 3.05 us
    transpose x1 -> x0, local copies, waits for them, and re-layouts: 2.43 us -> none  [body(): jnp.einsum('csr,vs->cvr', gathered, hadamard_table(devices), precision=la...]
where the time goes in v2:
time: 151 us; the launch traced here: 150 us
  blocking collectives  121 us (80%)
  Pallas kernels  25.9 us (17%)
  local copies, waits for them, and re-layouts  3.05 us (2%)
    all_to_all x1, blocking collectives, body(): lax.all_to_all(blocks, AXES, 0, 0, tiled=True).reshape(rows, columns, LANES)  63.9 us
    all_to_all x1, blocking collectives, body(): back = lax.all_to_all(mixed.reshape(blocks.shape), AXES, 0, 0, tiled=True)  56.8 us
    pallas_call x1, Pallas kernels, body(): y = vmem_call(pre_kernel, shape, 3)(x, signs, hadamard_table(LANES))  18.4 us
    pallas_call x1, Pallas kernels, body(): vmem_call(lambda a, b: mid_kernel(a, b, scale=scale), shape, 1)(gathered)  7.57 us
    unnamed x3, local copies, waits for them, and re-layouts  3.05 us

profile of v2, /device:TPU:0, one launch (start us, length us, event | category | flops | bytes accessed | tf_op | source)
XLA Modules:
  0.0 149.8 jit_solution(11823643679953025867)
XLA Ops:
  0.0 0.1 subtract_convert_fusion.h_ref
  0.1 0.0 copy-start
  0.1 1.0 copy-done
  1.1 18.4 %shard_map.28 = f32[1024,8,128]{2,1,0:T(8,128)S(1)} custom-call(f32[1024,8,128]{2,1,0:T(8,128)} %bitcast.17, s32[1024,128]{1,0:T(8,128)S(1)} %bitcast.14, f32[128,128]{1,0:T(8,128)S(1)} %subtract_convert_fusion.h_ref), custom_call_target="tpu_custom_call" | custom-call | tf_op jit(solution)/shard_map/pallas_call | solution.py:100
  19.5 63.9 %all_to_all.10 = f32[128,8,8,128]{3,2,1,0:T(8,128)} all-to-all(f32[128,8,8,128]{3,2,1,0:T(8,128)S(1)} %bitcast.12), channel_id=1, replica_groups=mesh['wide'=16,'narrow'=8] {'wide','narrow'}, dimensions={0} | all-to-all | bytes 8388608 | tf_op jit(solution)/shard_map/all_to_all | solution.py:102
  83.4 7.6 %shard_map.29 = f32[1024,8,128]{2,1,0:T(8,128)S(1)} custom-call(f32[1024,8,128]{2,1,0:T(8,128)} %bitcast.15), custom_call_target="tpu_custom_call" | custom-call | tf_op jit(solution)/shard_map/pallas_call | solution.py:104
  91.0 56.8 %all_to_all.11 = f32[128,8,8,128]{3,2,1,0:T(8,128)S(1)} all-to-all(f32[128,8,8,128]{3,2,1,0:T(8,128)S(1)} %bitcast.13), channel_id=1, replica_groups=mesh['wide'=16,'narrow'=8] {'wide','narrow'}, dimensions={0} | all-to-all | bytes 8388608 | tf_op jit(solution)/shard_map/all_to_all | solution.py:105
  147.8 2.0 %copy.4 = f32[8,131072]{1,0:T(8,128)} copy(f32[8,131072]{1,0:T(8,128)S(1)} %bitcast.16) | data formatting | bytes 8388608
Async XLA Ops:
  0.1 1.0 copy-start

commit v3 on v2

--- a/solution.py
+++ b/solution.py
@@ -1,3 +1,4 @@
+import functools
 import math
 
 import jax
@@ -54,38 +55,65 @@
     lax.fori_loop(0, rows // span, step, 0)
 
 
-def pre_kernel(x_ref, s_ref, h_ref, o_ref):
-    rows = x_ref.shape[0]
-    table = h_ref[...]
+CHUNKS = 8
+
+
+def split_rows(block):
+    high = block.astype(jnp.bfloat16)
+    rest = (block - high.astype(jnp.float32)).astype(jnp.bfloat16)
+    return jnp.concatenate([high, rest], axis=0)
+
+
+def chunked_kernel(x_hbm, *refs, inner, outer, signed):
+    if signed:
+        s_ref, h_ref, o_ref, buf, sems = refs
+    else:
+        o_ref, buf, sems = refs
+    rows = o_ref.shape[0]
+    size = rows // CHUNKS
+    copies = [
+        pltpu.make_async_copy(x_hbm.at[pl.ds(i * size, size)], buf.at[pl.ds(i * size, size)], sems.at[i])
+        for i in range(CHUNKS)
+    ]
+    for copy in copies:
+        copy.start()
 
     def signed_lanes(vals, base, stride):
+        table = h_ref[...]
+        cols = vals[0].shape[0]
         out = []
         for j, v in enumerate(vals):
             sign = s_ref[pl.ds(base + j * stride, 1), :].astype(jnp.float32) * 2.0 - 1.0
             out.append(v * sign)
         block = jnp.concatenate(out, axis=0)
-        mixed = jnp.dot(block, table, precision=lax.Precision.HIGHEST,
-                        preferred_element_type=jnp.float32)
-        cols = vals[0].shape[0]
+        both = jnp.dot(split_rows(block), table, preferred_element_type=jnp.float32)
+        count = block.shape[0]
+        mixed = both[:count] + both[count:]
         return [mixed[j * cols:(j + 1) * cols] for j in range(len(vals))]
 
-    radix_pass(x_ref, o_ref, rows, 3, 4, pre=signed_lanes)
-    radix_pass(o_ref, o_ref, rows, 7, 3)
+    for i, copy in enumerate(copies):
+        copy.wait()
+        src = buf.at[pl.ds(i * size, size)]
+        dst = o_ref.at[pl.ds(i * size, size)]
+        for n, (low, bits) in enumerate(inner):
+            pre = signed_lanes if (signed and n == 0) else None
+            if pre is not None:
+                offset = i * size
+                pre = (lambda f, o: (lambda vals, base, stride: f(vals, base + o, stride)))(signed_lanes, offset)
+            radix_pass(src if n == 0 else dst, dst, size, low, bits, pre=pre)
+    for n, (low, bits, post) in enumerate(outer):
+        radix_pass(o_ref, o_ref, rows, low, bits, post=post)
 
 
-def mid_kernel(x_ref, o_ref, *, scale):
-    rows = x_ref.shape[0]
-    radix_pass(x_ref, o_ref, rows, 0, 4)
-    radix_pass(o_ref, o_ref, rows, 4, 3)
-    radix_pass(o_ref, o_ref, rows, 7, 3, post=lambda v: v * scale)
-
-
-def vmem_call(kernel, out_shape, n_in):
+def chunked_call(out_shape, *, inner, outer, signed):
+    n_vmem = 2 if signed else 0
+    kernel = functools.partial(chunked_kernel, inner=inner, outer=outer, signed=signed)
     return pl.pallas_call(
         kernel,
         out_shape=out_shape,
-        in_specs=[pl.BlockSpec(memory_space=pltpu.VMEM)] * n_in,
+        in_specs=[pl.BlockSpec(memory_space=pl.ANY)] + [pl.BlockSpec(memory_space=pltpu.VMEM)] * n_vmem,
         out_specs=pl.BlockSpec(memory_space=pltpu.VMEM),
+        scratch_shapes=[pltpu.VMEM(out_shape.shape, jnp.float32), pltpu.SemaphoreType.DMA((CHUNKS,))],
         compiler_params=pltpu.CompilerParams(vmem_limit_bytes=48 * 1024 * 1024),
     )
 
@@ -97,11 +125,13 @@
     x = matrix_panel.reshape(columns, rows, LANES).transpose(1, 0, 2)
     signs = sign_bits.reshape(rows, LANES)
     shape = jax.ShapeDtypeStruct((rows, columns, LANES), jnp.float32)
-    y = vmem_call(pre_kernel, shape, 3)(x, signs, hadamard_table(LANES))
+    table = hadamard_table(LANES).astype(jnp.bfloat16)
+    y = chunked_call(shape, inner=((3, 4),), outer=((7, 3, None),), signed=True)(x, signs, table)
     blocks = y.reshape(devices, rows // devices, columns, LANES)
     gathered = lax.all_to_all(blocks, AXES, 0, 0, tiled=True).reshape(rows, columns, LANES)
     scale = 1.0 / math.sqrt(length * devices)
-    mixed = vmem_call(lambda a, b: mid_kernel(a, b, scale=scale), shape, 1)(gathered)
+    mid = chunked_call(shape, inner=((0, 4), (4, 3)), outer=((7, 3, lambda v: v * scale),), signed=False)
+    mixed = mid(gathered)
     back = lax.all_to_all(mixed.reshape(blocks.shape), AXES, 0, 0, tiled=True)
     return back.reshape(rows, columns, LANES).transpose(1, 0, 2).reshape(columns, length)
 

time: 151 us -> 145 us (0.960)
  Pallas kernels: 25.9 us -> 20.6 us
    pallas_call x2, Pallas kernels: 25.9 us -> 20.6 us  [the longest x1 14.1 us: body(): chunked_call(shape, inner=((3, 4),), outer=((7, 3, None),), signed=True)]
where the time goes in v3:
time: 145 us
  blocking collectives  121 us (83%)
  Pallas kernels  20.6 us (14%)
  local copies, waits for them, and re-layouts  3.05 us (2%)
    all_to_all x1, blocking collectives, body(): lax.all_to_all(blocks, AXES, 0, 0, tiled=True).reshape(rows, columns, LANES)  63.9 us
    all_to_all x1, blocking collectives, body(): back = lax.all_to_all(mixed.reshape(blocks.shape), AXES, 0, 0, tiled=True)  56.8 us
    pallas_call x1, Pallas kernels, body(): chunked_call(shape, inner=((3, 4),), outer=((7, 3, None),), signed=True)  14.1 us
    pallas_call x1, Pallas kernels, body(): mixed = mid(gathered)  6.5 us
    unnamed x3, local copies, waits for them, and re-layouts  3.05 us

profile of v3, /device:TPU:0, one launch (start us, length us, event | category | flops | bytes accessed | tf_op | source)
XLA Modules:
  0.0 144.5 jit_solution(15609856940457139607)
XLA Ops:
  0.0 0.1 convert_convert_fusion.refs_1_
  0.1 0.0 copy-start
  0.1 1.0 copy-done
  1.1 14.1 %shard_map.28 = f32[1024,8,128]{2,1,0:T(8,128)S(1)} custom-call(f32[1024,8,128]{2,1,0:T(8,128)} %bitcast.17, s32[1024,128]{1,0:T(8,128)S(1)} %bitcast.14, bf16[128,128]{1,0:T(8,128)(2,1)S(1)} %convert_convert_fusion.refs_1_), custom_call_target="tpu_custom_call" | custom-call | tf_op jit(solution)/shard_map/pallas_call | solution.py:129
  15.2 63.9 %all_to_all.10 = f32[128,8,8,128]{3,2,1,0:T(8,128)} all-to-all(f32[128,8,8,128]{3,2,1,0:T(8,128)S(1)} %bitcast.12), channel_id=1, replica_groups=mesh['wide'=16,'narrow'=8] {'wide','narrow'}, dimensions={0} | all-to-all | bytes 8388608 | tf_op jit(solution)/shard_map/all_to_all | solution.py:131
  79.1 6.5 %shard_map.29 = f32[1024,8,128]{2,1,0:T(8,128)S(1)} custom-call(f32[1024,8,128]{2,1,0:T(8,128)} %bitcast.15), custom_call_target="tpu_custom_call" | custom-call | tf_op jit(solution)/shard_map/pallas_call | solution.py:134
  85.7 56.8 %all_to_all.11 = f32[128,8,8,128]{3,2,1,0:T(8,128)S(1)} all-to-all(f32[128,8,8,128]{3,2,1,0:T(8,128)S(1)} %bitcast.13), channel_id=1, replica_groups=mesh['wide'=16,'narrow'=8] {'wide','narrow'}, dimensions={0} | all-to-all | bytes 8388608 | tf_op jit(solution)/shard_map/all_to_all | solution.py:135
  142.5 2.0 %copy.4 = f32[8,131072]{1,0:T(8,128)} copy(f32[8,131072]{1,0:T(8,128)S(1)} %bitcast.16) | data formatting | bytes 8388608
Async XLA Ops:
  0.1 1.0 copy-start

commit v4 on v3

--- a/solution.py
+++ b/solution.py
@@ -36,23 +36,14 @@
     return vals
 
 
-def radix_pass(src, dst, rows, low, bits, pre=None, post=None):
+def radix_pass(src, dst, rows, low, bits, post=None):
     span = 1 << bits
     stride = 1 << low
-
-    def step(g, carry):
+    for g in range(rows // span):
         base = (g // stride) * (stride * span) + g % stride
-        vals = [src[base + j * stride] for j in range(span)]
-        if pre is not None:
-            vals = pre(vals, base, stride)
-        vals = butterfly(vals)
-        if post is not None:
-            vals = [post(v) for v in vals]
+        vals = butterfly([src[base + j * stride] for j in range(span)])
         for j in range(span):
-            dst[base + j * stride] = vals[j]
-        return carry
-
-    lax.fori_loop(0, rows // span, step, 0)
+            dst[base + j * stride] = vals[j] if post is None else post(vals[j])
 
 
 CHUNKS = 8
@@ -78,29 +69,22 @@
     for copy in copies:
         copy.start()
 
-    def signed_lanes(vals, base, stride):
-        table = h_ref[...]
-        cols = vals[0].shape[0]
-        out = []
-        for j, v in enumerate(vals):
-            sign = s_ref[pl.ds(base + j * stride, 1), :].astype(jnp.float32) * 2.0 - 1.0
-            out.append(v * sign)
-        block = jnp.concatenate(out, axis=0)
-        both = jnp.dot(split_rows(block), table, preferred_element_type=jnp.float32)
-        count = block.shape[0]
-        mixed = both[:count] + both[count:]
-        return [mixed[j * cols:(j + 1) * cols] for j in range(len(vals))]
-
     for i, copy in enumerate(copies):
         copy.wait()
-        src = buf.at[pl.ds(i * size, size)]
-        dst = o_ref.at[pl.ds(i * size, size)]
+        rows_here = pl.ds(i * size, size)
+        dst = o_ref.at[rows_here]
+        if signed:
+            block = buf[rows_here]
+            sign = s_ref[rows_here, :].astype(jnp.float32) * 2.0 - 1.0
+            block = (block * sign[:, None, :]).reshape(size * block.shape[1], block.shape[2])
+            both = jnp.dot(split_rows(block), h_ref[...], preferred_element_type=jnp.float32)
+            count = block.shape[0]
+            dst[...] = (both[:count] + both[count:]).reshape(dst.shape)
+            first = dst
+        else:
+            first = buf.at[rows_here]
         for n, (low, bits) in enumerate(inner):
-            pre = signed_lanes if (signed and n == 0) else None
-            if pre is not None:
-                offset = i * size
-                pre = (lambda f, o: (lambda vals, base, stride: f(vals, base + o, stride)))(signed_lanes, offset)
-            radix_pass(src if n == 0 else dst, dst, size, low, bits, pre=pre)
+            radix_pass(first if n == 0 else dst, dst, size, low, bits)
     for n, (low, bits, post) in enumerate(outer):
         radix_pass(o_ref, o_ref, rows, low, bits, post=post)
 

time: 145 us -> 133 us (0.917)
  Pallas kernels: 20.6 us -> 8.64 us
    pallas_call x1, Pallas kernels: 14.1 us -> 5.68 us  [body(): chunked_call(shape, inner=((3, 4),), outer=((7, 3, None),), signed=True)]
    pallas_call x1, Pallas kernels: 6.5 us -> 2.95 us  [body(): mixed = mid(gathered)]
where the time goes in v4:
time: 133 us
  blocking collectives  121 us (91%)
  Pallas kernels  8.64 us (6%)
  local copies, waits for them, and re-layouts  3.05 us (2%)
    all_to_all x1, blocking collectives, body(): lax.all_to_all(blocks, AXES, 0, 0, tiled=True).reshape(rows, columns, LANES)  63.9 us
    all_to_all x1, blocking collectives, body(): back = lax.all_to_all(mixed.reshape(blocks.shape), AXES, 0, 0, tiled=True)  56.8 us
    pallas_call x1, Pallas kernels, body(): chunked_call(shape, inner=((3, 4),), outer=((7, 3, None),), signed=True)  5.68 us
    unnamed x3, local copies, waits for them, and re-layouts  3.05 us
    pallas_call x1, Pallas kernels, body(): mixed = mid(gathered)  2.95 us

profile of v4, /device:TPU:0, one launch (start us, length us, event | category | flops | bytes accessed | tf_op | source)
XLA Modules:
  0.0 132.5 jit_solution(15849965659502742108)
XLA Ops:
  0.0 0.1 convert_convert_fusion.refs_1_
  0.1 0.0 copy-start
  0.1 1.0 copy-done
  1.1 5.7 %shard_map.28 = f32[1024,8,128]{2,1,0:T(8,128)S(1)} custom-call(f32[1024,8,128]{2,1,0:T(8,128)} %bitcast.17, s32[1024,128]{1,0:T(8,128)S(1)} %bitcast.14, bf16[128,128]{1,0:T(8,128)(2,1)S(1)} %convert_convert_fusion.refs_1_), custom_call_target="tpu_custom_call" | custom-call | tf_op jit(solution)/shard_map/pallas_call | solution.py:113
  6.8 63.9 %all_to_all.10 = f32[128,8,8,128]{3,2,1,0:T(8,128)} all-to-all(f32[128,8,8,128]{3,2,1,0:T(8,128)S(1)} %bitcast.12), channel_id=1, replica_groups=mesh['wide'=16,'narrow'=8] {'wide','narrow'}, dimensions={0} | all-to-all | bytes 8388608 | tf_op jit(solution)/shard_map/all_to_all | solution.py:115
  70.7 3.0 %shard_map.29 = f32[1024,8,128]{2,1,0:T(8,128)S(1)} custom-call(f32[1024,8,128]{2,1,0:T(8,128)} %bitcast.15), custom_call_target="tpu_custom_call" | custom-call | tf_op jit(solution)/shard_map/pallas_call | solution.py:118
  73.7 56.8 %all_to_all.11 = f32[128,8,8,128]{3,2,1,0:T(8,128)S(1)} all-to-all(f32[128,8,8,128]{3,2,1,0:T(8,128)S(1)} %bitcast.13), channel_id=1, replica_groups=mesh['wide'=16,'narrow'=8] {'wide','narrow'}, dimensions={0} | all-to-all | bytes 8388608 | tf_op jit(solution)/shard_map/all_to_all | solution.py:119
  130.5 2.0 %copy.4 = f32[8,131072]{1,0:T(8,128)} copy(f32[8,131072]{1,0:T(8,128)S(1)} %bitcast.16) | data formatting | bytes 8388608
Async XLA Ops:
  0.1 1.0 copy-start

commit v5 on v4

--- a/solution.py
+++ b/solution.py
@@ -9,6 +9,7 @@
 from jax.sharding import PartitionSpec as P
 
 AXES = ("wide", "narrow")
+GROUP = ("narrow", "wide")
 LANES = 128
 
 
@@ -112,11 +113,11 @@
     table = hadamard_table(LANES).astype(jnp.bfloat16)
     y = chunked_call(shape, inner=((3, 4),), outer=((7, 3, None),), signed=True)(x, signs, table)
     blocks = y.reshape(devices, rows // devices, columns, LANES)
-    gathered = lax.all_to_all(blocks, AXES, 0, 0, tiled=True).reshape(rows, columns, LANES)
+    gathered = lax.all_to_all(blocks, GROUP, 0, 0, tiled=True).reshape(rows, columns, LANES)
     scale = 1.0 / math.sqrt(length * devices)
     mid = chunked_call(shape, inner=((0, 4), (4, 3)), outer=((7, 3, lambda v: v * scale),), signed=False)
     mixed = mid(gathered)
-    back = lax.all_to_all(mixed.reshape(blocks.shape), AXES, 0, 0, tiled=True)
+    back = lax.all_to_all(mixed.reshape(blocks.shape), GROUP, 0, 0, tiled=True)
     return back.reshape(rows, columns, LANES).transpose(1, 0, 2).reshape(columns, length)
 
 

time: 133 us -> 132 us (level)
  no operation moved by 1% of the time
where the time goes in v5:
time: 132 us; the launch traced here: 131 us
  blocking collectives  120 us (91%)
  Pallas kernels  8.64 us (7%)
  local copies, waits for them, and re-layouts  3.05 us (2%)
    all_to_all x1, blocking collectives, body(): lax.all_to_all(blocks, GROUP, 0, 0, tiled=True)  62.9 us
    all_to_all x1, blocking collectives, body(): back = lax.all_to_all(mixed.reshape(blocks.shape), GROUP, 0, 0, tiled=True)  56.6 us
    pallas_call x1, Pallas kernels, body(): chunked_call(shape, inner=((3, 4),), outer=((7, 3, None),), signed=True)  5.68 us
    unnamed x3, local copies, waits for them, and re-layouts  3.05 us
    pallas_call x1, Pallas kernels, body(): mixed = mid(gathered)  2.95 us

profile of v5, /device:TPU:0, one launch (start us, length us, event | category | flops | bytes accessed | tf_op | source)
XLA Modules:
  0.0 131.3 jit_solution(10961336577402002931)
XLA Ops:
  0.0 0.1 convert_convert_fusion.refs_1_
  0.1 0.0 copy-start
  0.1 1.0 copy-done
  1.1 5.7 %shard_map.28 = f32[1024,8,128]{2,1,0:T(8,128)S(1)} custom-call(f32[1024,8,128]{2,1,0:T(8,128)} %bitcast.17, s32[1024,128]{1,0:T(8,128)S(1)} %bitcast.14, bf16[128,128]{1,0:T(8,128)(2,1)S(1)} %convert_convert_fusion.refs_1_), custom_call_target="tpu_custom_call" | custom-call | tf_op jit(solution)/shard_map/pallas_call | solution.py:114
  6.8 62.9 %all_to_all.10 = f32[128,8,8,128]{3,2,1,0:T(8,128)} all-to-all(f32[128,8,8,128]{3,2,1,0:T(8,128)S(1)} %bitcast.12), channel_id=1, replica_groups=mesh['wide'=16,'narrow'=8] {'narrow','wide'}, dimensions={0} | all-to-all | bytes 8388608 | tf_op jit(solution)/shard_map/all_to_all | solution.py:116
  69.7 3.0 %shard_map.29 = f32[1024,8,128]{2,1,0:T(8,128)S(1)} custom-call(f32[1024,8,128]{2,1,0:T(8,128)} %bitcast.15), custom_call_target="tpu_custom_call" | custom-call | tf_op jit(solution)/shard_map/pallas_call | solution.py:119
  72.7 56.6 %all_to_all.11 = f32[128,8,8,128]{3,2,1,0:T(8,128)S(1)} all-to-all(f32[128,8,8,128]{3,2,1,0:T(8,128)S(1)} %bitcast.13), channel_id=1, replica_groups=mesh['wide'=16,'narrow'=8] {'narrow','wide'}, dimensions={0} | all-to-all | bytes 8388608 | tf_op jit(solution)/shard_map/all_to_all | solution.py:120
  129.3 2.0 %copy.4 = f32[8,131072]{1,0:T(8,128)} copy(f32[8,131072]{1,0:T(8,128)S(1)} %bitcast.16) | data formatting | bytes 8388608
Async XLA Ops:
  0.1 1.0 copy-start

commit v6 on v5

--- a/solution.py
+++ b/solution.py
@@ -56,6 +56,48 @@
     return jnp.concatenate([high, rest], axis=0)
 
 
+def pre_kernel(x_hbm, s_ref, h_ref, o_ref, buf, sems):
+    blocks, chunks, cols, lanes = o_ref.shape
+    copies = [
+        pltpu.make_async_copy(x_hbm.at[:, i], buf.at[i], sems.at[i]) for i in range(chunks)
+    ]
+    for copy in copies:
+        copy.start()
+    low = 16
+    for i, copy in enumerate(copies):
+        copy.wait()
+        block = buf[i]
+        sign = s_ref[pl.ds(i, blocks, stride=chunks), :].astype(jnp.float32) * 2.0 - 1.0
+        block = (block * sign[:, None, :]).reshape(blocks * cols, lanes)
+        both = jnp.dot(split_rows(block), h_ref[...], preferred_element_type=jnp.float32)
+        count = blocks * cols
+        for g in range(blocks // low):
+            vals = []
+            for j in range(low):
+                r = (g * low + j) * cols
+                vals.append(both[r:r + cols] + both[count + r:count + r + cols])
+            vals = butterfly(vals)
+            for j in range(low):
+                o_ref[g * low + j, i] = vals[j]
+        for j in range(low):
+            vals = butterfly([o_ref[g * low + j, i] for g in range(blocks // low)])
+            for g in range(blocks // low):
+                o_ref[g * low + j, i] = vals[g]
+
+
+def pre_call(out_shape):
+    blocks, chunks, cols, lanes = out_shape.shape
+    return pl.pallas_call(
+        pre_kernel,
+        out_shape=out_shape,
+        in_specs=[pl.BlockSpec(memory_space=pl.ANY)] + [pl.BlockSpec(memory_space=pltpu.VMEM)] * 2,
+        out_specs=pl.BlockSpec(memory_space=pltpu.VMEM),
+        scratch_shapes=[pltpu.VMEM((chunks, blocks, cols, lanes), jnp.float32),
+                        pltpu.SemaphoreType.DMA((chunks,))],
+        compiler_params=pltpu.CompilerParams(vmem_limit_bytes=48 * 1024 * 1024),
+    )
+
+
 def chunked_kernel(x_hbm, *refs, inner, outer, signed):
     if signed:
         s_ref, h_ref, o_ref, buf, sems = refs
@@ -111,8 +153,8 @@
     signs = sign_bits.reshape(rows, LANES)
     shape = jax.ShapeDtypeStruct((rows, columns, LANES), jnp.float32)
     table = hadamard_table(LANES).astype(jnp.bfloat16)
-    y = chunked_call(shape, inner=((3, 4),), outer=((7, 3, None),), signed=True)(x, signs, table)
-    blocks = y.reshape(devices, rows // devices, columns, LANES)
+    block_shape = jax.ShapeDtypeStruct((devices, rows // devices, columns, LANES), jnp.float32)
+    blocks = pre_call(block_shape)(x.reshape(block_shape.shape), signs, table)
     gathered = lax.all_to_all(blocks, GROUP, 0, 0, tiled=True).reshape(rows, columns, LANES)
     scale = 1.0 / math.sqrt(length * devices)
     mid = chunked_call(shape, inner=((0, 4), (4, 3)), outer=((7, 3, lambda v: v * scale),), signed=False)

time: 132 us -> 131 us (level)
  no operation moved by 1% of the time
where the time goes in v6:
time: 131 us
  blocking collectives  120 us (92%)
  Pallas kernels  8.06 us (6%)
  local copies, waits for them, and re-layouts  3.05 us (2%)
    all_to_all x1, blocking collectives, body(): lax.all_to_all(blocks, GROUP, 0, 0, tiled=True)  62.9 us
    all_to_all x1, blocking collectives, body(): back = lax.all_to_all(mixed.reshape(blocks.shape), GROUP, 0, 0, tiled=True)  56.6 us
    pallas_call x1, Pallas kernels, body(): blocks = pre_call(block_shape)(x.reshape(block_shape.shape), signs, table)  5.11 us
    unnamed x3, local copies, waits for them, and re-layouts  3.05 us
    pallas_call x1, Pallas kernels, body(): mixed = mid(gathered)  2.95 us

profile of v6, /device:TPU:0, one launch (start us, length us, event | category | flops | bytes accessed | tf_op | source)
XLA Modules:
  0.0 130.8 jit_solution(13972583680646571993)
XLA Ops:
  0.0 0.1 convert_convert_fusion.h_ref
  0.1 0.0 copy-start
  0.1 1.0 copy-done
  1.1 5.1 %shard_map.28 = f32[128,8,8,128]{3,2,1,0:T(8,128)S(1)} custom-call(f32[128,8,8,128]{3,2,1,0:T(8,128)} %bitcast.17, s32[1024,128]{1,0:T(8,128)S(1)} %bitcast.14, bf16[128,128]{1,0:T(8,128)(2,1)S(1)} %convert_convert_fusion.h_ref), custom_call_target="tpu_custom_call" | custom-call | tf_op jit(solution)/shard_map/pallas_call | solution.py:157
  6.2 62.9 %all_to_all.10 = f32[128,8,8,128]{3,2,1,0:T(8,128)} all-to-all(f32[128,8,8,128]{3,2,1,0:T(8,128)S(1)} %shard_map.28), channel_id=1, replica_groups=mesh['wide'=16,'narrow'=8] {'narrow','wide'}, dimensions={0} | all-to-all | bytes 8388608 | tf_op jit(solution)/shard_map/all_to_all | solution.py:158
  69.1 3.0 %shard_map.29 = f32[1024,8,128]{2,1,0:T(8,128)S(1)} custom-call(f32[1024,8,128]{2,1,0:T(8,128)} %bitcast.15), custom_call_target="tpu_custom_call" | custom-call | tf_op jit(solution)/shard_map/pallas_call | solution.py:161
  72.1 56.6 %all_to_all.11 = f32[128,8,8,128]{3,2,1,0:T(8,128)S(1)} all-to-all(f32[128,8,8,128]{3,2,1,0:T(8,128)S(1)} %bitcast.13), channel_id=1, replica_groups=mesh['wide'=16,'narrow'=8] {'narrow','wide'}, dimensions={0} | all-to-all | bytes 8388608 | tf_op jit(solution)/shard_map/all_to_all | solution.py:162
  128.7 2.0 %copy.4 = f32[8,131072]{1,0:T(8,128)} copy(f32[8,131072]{1,0:T(8,128)S(1)} %bitcast.16) | data formatting | bytes 8388608
Async XLA Ops:
  0.1 1.0 copy-start

commit v7 on v6

--- a/solution.py
+++ b/solution.py
@@ -94,7 +94,7 @@
         out_specs=pl.BlockSpec(memory_space=pltpu.VMEM),
         scratch_shapes=[pltpu.VMEM((chunks, blocks, cols, lanes), jnp.float32),
                         pltpu.SemaphoreType.DMA((chunks,))],
-        compiler_params=pltpu.CompilerParams(vmem_limit_bytes=48 * 1024 * 1024),
+        compiler_params=pltpu.CompilerParams(vmem_limit_bytes=24 * 1024 * 1024),
     )
 
 
@@ -141,7 +141,7 @@
         in_specs=[pl.BlockSpec(memory_space=pl.ANY)] + [pl.BlockSpec(memory_space=pltpu.VMEM)] * n_vmem,
         out_specs=pl.BlockSpec(memory_space=pltpu.VMEM),
         scratch_shapes=[pltpu.VMEM(out_shape.shape, jnp.float32), pltpu.SemaphoreType.DMA((CHUNKS,))],
-        compiler_params=pltpu.CompilerParams(vmem_limit_bytes=48 * 1024 * 1024),
+        compiler_params=pltpu.CompilerParams(vmem_limit_bytes=24 * 1024 * 1024),
     )
 
 

time: 131 us -> 132 us (level)
  local copies, waits for them, and re-layouts: 3.05 us -> 5.24 us
  Pallas kernels: 8.06 us -> 6.7 us
    unnamed x3 -> x5, local copies, waits for them, and re-layouts: 3.05 us -> 5.24 us
where the time goes in v7:
time: 132 us; the launch traced here: 131 us
  blocking collectives  119 us (90%)
  Pallas kernels  6.7 us (5%)
  local copies, waits for them, and re-layouts  5.24 us (4%)
    all_to_all x1, blocking collectives, body(): lax.all_to_all(blocks, GROUP, 0, 0, tiled=True)  62.8 us
    all_to_all x1, blocking collectives, body(): back = lax.all_to_all(mixed.reshape(blocks.shape), GROUP, 0, 0, tiled=True)  56.7 us
    unnamed x5, local copies, waits for them, and re-layouts  5.24 us
    pallas_call x1, Pallas kernels, body(): blocks = pre_call(block_shape)(x.reshape(block_shape.shape), signs, table)  4.66 us

profile of v7, /device:TPU:0, one launch (start us, length us, event | category | flops | bytes accessed | tf_op | source)
XLA Modules:
  0.0 131.5 jit_solution(2904291323566295663)
XLA Ops:
  0.0 0.1 convert_convert_fusion.h_ref
  0.1 0.0 copy-start
  0.1 2.2 %copy-done = f32[8,131072]{1,0:T(8,128)S(1)} copy-done((f32[8,131072]{1,0:T(8,128)S(1)}, f32[8,131072]{1,0:T(8,128)}, u32[]{:S(2)}) %copy-start) | copy-done | bytes 4194328
  2.3 0.0 copy-start.1
  2.3 1.0 copy-done.1
  3.3 4.7 %shard_map.28 = f32[128,8,8,128]{3,2,1,0:T(8,128)S(1)} custom-call(f32[128,8,8,128]{3,2,1,0:T(8,128)S(1)} %bitcast.15, s32[1024,128]{1,0:T(8,128)S(1)} %bitcast.16, bf16[128,128]{1,0:T(8,128)(2,1)S(1)} %convert_convert_fusion.h_ref), custom_call_target="tpu_custom_call" | custom-call | tf_op jit(solution)/shard_map/pallas_call | solution.py:157
  8.0 62.8 %all_to_all.10 = f32[128,8,8,128]{3,2,1,0:T(8,128)S(1)} all-to-all(f32[128,8,8,128]{3,2,1,0:T(8,128)S(1)} %shard_map.28), channel_id=1, replica_groups=mesh['wide'=16,'narrow'=8] {'narrow','wide'}, dimensions={0} | all-to-all | bytes 8388608 | tf_op jit(solution)/shard_map/all_to_all | solution.py:158
  70.8 2.0 %shard_map.29 = f32[1024,8,128]{2,1,0:T(8,128)S(1)} custom-call(f32[1024,8,128]{2,1,0:T(8,128)S(1)} %bitcast.13), custom_call_target="tpu_custom_call" | custom-call | tf_op jit(solution)/shard_map/pallas_call | solution.py:161
  72.8 56.7 %all_to_all.11 = f32[128,8,8,128]{3,2,1,0:T(8,128)S(1)} all-to-all(f32[128,8,8,128]{3,2,1,0:T(8,128)S(1)} %bitcast.14), channel_id=1, replica_groups=mesh['wide'=16,'narrow'=8] {'narrow','wide'}, dimensions={0} | all-to-all | bytes 8388608 | tf_op jit(solution)/shard_map/all_to_all | solution.py:162
  129.5 2.0 %copy.4 = f32[8,131072]{1,0:T(8,128)} copy(f32[8,131072]{1,0:T(8,128)S(1)} %bitcast.17) | data formatting | bytes 8388608
Async XLA Ops:
  0.1 2.2 %copy-start = (f32[8,131072]{1,0:T(8,128)S(1)}, f32[8,131072]{1,0:T(8,128)}, u32[]{:S(2)}) copy-start(f32[8,131072]{1,0:T(8,128)} %param.2) | copy-start | bytes 12582916
  2.3 1.0 copy-start.1

commit v8 on v6

--- a/solution.py
+++ b/solution.py
@@ -141,7 +141,7 @@
         in_specs=[pl.BlockSpec(memory_space=pl.ANY)] + [pl.BlockSpec(memory_space=pltpu.VMEM)] * n_vmem,
         out_specs=pl.BlockSpec(memory_space=pltpu.VMEM),
         scratch_shapes=[pltpu.VMEM(out_shape.shape, jnp.float32), pltpu.SemaphoreType.DMA((CHUNKS,))],
-        compiler_params=pltpu.CompilerParams(vmem_limit_bytes=48 * 1024 * 1024),
+        compiler_params=pltpu.CompilerParams(vmem_limit_bytes=16 * 1024 * 1024),
     )
 
 

time: 131 us -> 130 us (level)
  no operation moved by 1% of the time
where the time goes in v8:
time: 130 us
  blocking collectives  119 us (92%)
  Pallas kernels  7.15 us (6%)
  local copies, waits for them, and re-layouts  3.05 us (2%)
    all_to_all x1, blocking collectives, body(): lax.all_to_all(blocks, GROUP, 0, 0, tiled=True)  62.8 us
    all_to_all x1, blocking collectives, body(): back = lax.all_to_all(mixed.reshape(blocks.shape), GROUP, 0, 0, tiled=True)  56.7 us
    pallas_call x1, Pallas kernels, body(): blocks = pre_call(block_shape)(x.reshape(block_shape.shape), signs, table)  5.11 us
    unnamed x3, local copies, waits for them, and re-layouts  3.05 us

profile of v8, /device:TPU:0, one launch (start us, length us, event | category | flops | bytes accessed | tf_op | source)
XLA Modules:
  0.0 129.7 jit_solution(4319402995008994783)
XLA Ops:
  0.0 0.1 convert_convert_fusion.h_ref
  0.1 0.0 copy-start
  0.1 1.0 copy-done
  1.1 5.1 %shard_map.28 = f32[128,8,8,128]{3,2,1,0:T(8,128)S(1)} custom-call(f32[128,8,8,128]{3,2,1,0:T(8,128)} %bitcast.17, s32[1024,128]{1,0:T(8,128)S(1)} %bitcast.15, bf16[128,128]{1,0:T(8,128)(2,1)S(1)} %convert_convert_fusion.h_ref), custom_call_target="tpu_custom_call" | custom-call | tf_op jit(solution)/shard_map/pallas_call | solution.py:157
  6.2 62.8 %all_to_all.10 = f32[128,8,8,128]{3,2,1,0:T(8,128)S(1)} all-to-all(f32[128,8,8,128]{3,2,1,0:T(8,128)S(1)} %shard_map.28), channel_id=1, replica_groups=mesh['wide'=16,'narrow'=8] {'narrow','wide'}, dimensions={0} | all-to-all | bytes 8388608 | tf_op jit(solution)/shard_map/all_to_all | solution.py:158
  69.0 2.0 %shard_map.29 = f32[1024,8,128]{2,1,0:T(8,128)S(1)} custom-call(f32[1024,8,128]{2,1,0:T(8,128)S(1)} %bitcast.13), custom_call_target="tpu_custom_call" | custom-call | tf_op jit(solution)/shard_map/pallas_call | solution.py:161
  71.1 56.7 %all_to_all.11 = f32[128,8,8,128]{3,2,1,0:T(8,128)S(1)} all-to-all(f32[128,8,8,128]{3,2,1,0:T(8,128)S(1)} %bitcast.14), channel_id=1, replica_groups=mesh['wide'=16,'narrow'=8] {'narrow','wide'}, dimensions={0} | all-to-all | bytes 8388608 | tf_op jit(solution)/shard_map/all_to_all | solution.py:162
  127.7 2.0 %copy.4 = f32[8,131072]{1,0:T(8,128)} copy(f32[8,131072]{1,0:T(8,128)S(1)} %bitcast.16) | data formatting | bytes 8388608
Async XLA Ops:
  0.1 1.0 copy-start

commit v9 on v8

--- a/solution.py
+++ b/solution.py
@@ -56,13 +56,19 @@
     return jnp.concatenate([high, rest], axis=0)
 
 
-def pre_kernel(x_hbm, s_ref, h_ref, o_ref, buf, sems):
-    blocks, chunks, cols, lanes = o_ref.shape
+def pre_kernel(x_hbm, s_hbm, h_ref, o_hbm, buf, s_ref, obuf, sems, out_sems):
+    blocks, chunks, cols, lanes = o_hbm.shape
+    sign_copy = pltpu.make_async_copy(s_hbm, s_ref, sems.at[chunks])
     copies = [
         pltpu.make_async_copy(x_hbm.at[:, i], buf.at[i], sems.at[i]) for i in range(chunks)
     ]
+    outs = [
+        pltpu.make_async_copy(obuf.at[i], o_hbm.at[:, i], out_sems.at[i]) for i in range(chunks)
+    ]
+    sign_copy.start()
     for copy in copies:
         copy.start()
+    sign_copy.wait()
     low = 16
     for i, copy in enumerate(copies):
         copy.wait()
@@ -71,6 +77,7 @@
         block = (block * sign[:, None, :]).reshape(blocks * cols, lanes)
         both = jnp.dot(split_rows(block), h_ref[...], preferred_element_type=jnp.float32)
         count = blocks * cols
+        dst = obuf.at[i]
         for g in range(blocks // low):
             vals = []
             for j in range(low):
@@ -78,11 +85,14 @@
                 vals.append(both[r:r + cols] + both[count + r:count + r + cols])
             vals = butterfly(vals)
             for j in range(low):
-                o_ref[g * low + j, i] = vals[j]
+                dst[g * low + j] = vals[j]
         for j in range(low):
-            vals = butterfly([o_ref[g * low + j, i] for g in range(blocks // low)])
+            vals = butterfly([dst[g * low + j] for g in range(blocks // low)])
             for g in range(blocks // low):
-                o_ref[g * low + j, i] = vals[g]
+                dst[g * low + j] = vals[g]
+        outs[i].start()
+    for out in outs:
+        out.wait()
 
 
 def pre_call(out_shape):
@@ -90,11 +100,14 @@
     return pl.pallas_call(
         pre_kernel,
         out_shape=out_shape,
-        in_specs=[pl.BlockSpec(memory_space=pl.ANY)] + [pl.BlockSpec(memory_space=pltpu.VMEM)] * 2,
-        out_specs=pl.BlockSpec(memory_space=pltpu.VMEM),
+        in_specs=[pl.BlockSpec(memory_space=pl.ANY)] * 2 + [pl.BlockSpec(memory_space=pltpu.VMEM)],
+        out_specs=pl.BlockSpec(memory_space=pl.ANY),
         scratch_shapes=[pltpu.VMEM((chunks, blocks, cols, lanes), jnp.float32),
+                        pltpu.VMEM((blocks * chunks, lanes), jnp.int32),
+                        pltpu.VMEM((chunks, blocks, cols, lanes), jnp.float32),
+                        pltpu.SemaphoreType.DMA((chunks + 1,)),
                         pltpu.SemaphoreType.DMA((chunks,))],
-        compiler_params=pltpu.CompilerParams(vmem_limit_bytes=48 * 1024 * 1024),
+        compiler_params=pltpu.CompilerParams(vmem_limit_bytes=56 * 1024 * 1024),
     )
 
 

time: 130 us -> 131 us (level)
  Pallas kernels: 7.15 us -> 8.56 us
    pallas_call x1, Pallas kernels: 5.11 us -> 6.51 us  [body(): blocks = pre_call(block_shape)(x.reshape(block_shape.shape), signs, table)]
    unnamed x3 -> x1, local copies, waits for them, and re-layouts: 3.05 us -> 2.01 us
where the time goes in v9:
time: 131 us
  blocking collectives  120 us (92%)
  Pallas kernels  8.56 us (7%)
  local copies, waits for them, and re-layouts  2.01 us (2%)
    all_to_all x1, blocking collectives, body(): lax.all_to_all(blocks, GROUP, 0, 0, tiled=True)  63 us
    all_to_all x1, blocking collectives, body(): back = lax.all_to_all(mixed.reshape(blocks.shape), GROUP, 0, 0, tiled=True)  56.7 us
    pallas_call x1, Pallas kernels, body(): blocks = pre_call(block_shape)(x.reshape(block_shape.shape), signs, table)  6.51 us

profile of v9, /device:TPU:0, one launch (start us, length us, event | category | flops | bytes accessed | tf_op | source)
XLA Modules:
  0.0 130.9 jit_solution(5433878269759061030)
XLA Ops:
  0.0 0.7 convert_convert_fusion.h_ref
  0.7 6.5 %shard_map.28 = f32[128,8,8,128]{3,2,1,0:T(8,128)} custom-call(f32[128,8,8,128]{3,2,1,0:T(8,128)} %bitcast.16, s32[1024,128]{1,0:T(8,128)} %bitcast.17, bf16[128,128]{1,0:T(8,128)(2,1)} %convert_convert_fusion.h_ref), custom_call_target="tpu_custom_call" | custom-call | tf_op jit(solution)/shard_map/pallas_call | solution.py:170
  7.2 63.0 %all_to_all.10 = f32[128,8,8,128]{3,2,1,0:T(8,128)S(1)} all-to-all(f32[128,8,8,128]{3,2,1,0:T(8,128)} %shard_map.28), channel_id=1, replica_groups=mesh['wide'=16,'narrow'=8] {'narrow','wide'}, dimensions={0} | all-to-all | bytes 8388608 | tf_op jit(solution)/shard_map/all_to_all | solution.py:171
  70.2 2.0 %shard_map.29 = f32[1024,8,128]{2,1,0:T(8,128)S(1)} custom-call(f32[1024,8,128]{2,1,0:T(8,128)S(1)} %bitcast.13), custom_call_target="tpu_custom_call" | custom-call | tf_op jit(solution)/shard_map/pallas_call | solution.py:174
  72.2 56.7 %all_to_all.11 = f32[128,8,8,128]{3,2,1,0:T(8,128)S(1)} all-to-all(f32[128,8,8,128]{3,2,1,0:T(8,128)S(1)} %bitcast.14), channel_id=1, replica_groups=mesh['wide'=16,'narrow'=8] {'narrow','wide'}, dimensions={0} | all-to-all | bytes 8388608 | tf_op jit(solution)/shard_map/all_to_all | solution.py:175
  128.9 2.0 %copy.4 = f32[8,131072]{1,0:T(8,128)} copy(f32[8,131072]{1,0:T(8,128)S(1)} %bitcast.15) | data formatting | bytes 8388608

commit v10 on v8

--- a/solution.py
+++ b/solution.py
@@ -11,6 +11,8 @@
 AXES = ("wide", "narrow")
 GROUP = ("narrow", "wide")
 LANES = 128
+LIFT_BITS = 64
+LIFT = float(2.0 ** LIFT_BITS)
 
 
 def hadamard_table(order):
@@ -67,7 +69,7 @@
     for i, copy in enumerate(copies):
         copy.wait()
         block = buf[i]
-        sign = s_ref[pl.ds(i, blocks, stride=chunks), :].astype(jnp.float32) * 2.0 - 1.0
+        sign = (s_ref[pl.ds(i, blocks, stride=chunks), :].astype(jnp.float32) * 2.0 - 1.0) * LIFT
         block = (block * sign[:, None, :]).reshape(blocks * cols, lanes)
         both = jnp.dot(split_rows(block), h_ref[...], preferred_element_type=jnp.float32)
         count = blocks * cols
@@ -156,7 +158,7 @@
     block_shape = jax.ShapeDtypeStruct((devices, rows // devices, columns, LANES), jnp.float32)
     blocks = pre_call(block_shape)(x.reshape(block_shape.shape), signs, table)
     gathered = lax.all_to_all(blocks, GROUP, 0, 0, tiled=True).reshape(rows, columns, LANES)
-    scale = 1.0 / math.sqrt(length * devices)
+    scale = 2.0 ** -LIFT_BITS / math.sqrt(length * devices)
     mid = chunked_call(shape, inner=((0, 4), (4, 3)), outer=((7, 3, lambda v: v * scale),), signed=False)
     mixed = mid(gathered)
     back = lax.all_to_all(mixed.reshape(blocks.shape), GROUP, 0, 0, tiled=True)

time: 130 us -> 130 us (level)
  no operation moved by 1% of the time
where the time goes in v10:
time: 130 us
  blocking collectives  119 us (92%)
  Pallas kernels  7.15 us (6%)
  local copies, waits for them, and re-layouts  3.05 us (2%)
    all_to_all x1, blocking collectives, body(): lax.all_to_all(blocks, GROUP, 0, 0, tiled=True)  62.8 us
    all_to_all x1, blocking collectives, body(): back = lax.all_to_all(mixed.reshape(blocks.shape), GROUP, 0, 0, tiled=True)  56.7 us
    pallas_call x1, Pallas kernels, body(): blocks = pre_call(block_shape)(x.reshape(block_shape.shape), signs, table)  5.11 us
    unnamed x3, local copies, waits for them, and re-layouts  3.05 us

profile of v10, /device:TPU:0, one launch (start us, length us, event | category | flops | bytes accessed | tf_op | source)
XLA Modules:
  0.0 129.7 jit_solution(11862043842759067965)
XLA Ops:
  0.0 0.1 convert_convert_fusion.h_ref
  0.1 0.0 copy-start
  0.1 1.0 copy-done
  1.1 5.1 %shard_map.28 = f32[128,8,8,128]{3,2,1,0:T(8,128)S(1)} custom-call(f32[128,8,8,128]{3,2,1,0:T(8,128)} %bitcast.17, s32[1024,128]{1,0:T(8,128)S(1)} %bitcast.15, bf16[128,128]{1,0:T(8,128)(2,1)S(1)} %convert_convert_fusion.h_ref), custom_call_target="tpu_custom_call" | custom-call | tf_op jit(solution)/shard_map/pallas_call | solution.py:159
  6.2 62.8 %all_to_all.10 = f32[128,8,8,128]{3,2,1,0:T(8,128)S(1)} all-to-all(f32[128,8,8,128]{3,2,1,0:T(8,128)S(1)} %shard_map.28), channel_id=1, replica_groups=mesh['wide'=16,'narrow'=8] {'narrow','wide'}, dimensions={0} | all-to-all | bytes 8388608 | tf_op jit(solution)/shard_map/all_to_all | solution.py:160
  69.0 2.0 %shard_map.29 = f32[1024,8,128]{2,1,0:T(8,128)S(1)} custom-call(f32[1024,8,128]{2,1,0:T(8,128)S(1)} %bitcast.13), custom_call_target="tpu_custom_call" | custom-call | tf_op jit(solution)/shard_map/pallas_call | solution.py:163
  71.1 56.7 %all_to_all.11 = f32[128,8,8,128]{3,2,1,0:T(8,128)S(1)} all-to-all(f32[128,8,8,128]{3,2,1,0:T(8,128)S(1)} %bitcast.14), channel_id=1, replica_groups=mesh['wide'=16,'narrow'=8] {'narrow','wide'}, dimensions={0} | all-to-all | bytes 8388608 | tf_op jit(solution)/shard_map/all_to_all | solution.py:164
  127.7 2.0 %copy.4 = f32[8,131072]{1,0:T(8,128)} copy(f32[8,131072]{1,0:T(8,128)S(1)} %bitcast.16) | data formatting | bytes 8388608
Async XLA Ops:
  0.1 1.0 copy-start
